TPU v7x, 512 devices: a whole 4x4x16 slice. The times are simulated.
512 devices in a mesh: seq: 128 (over z, x, core), fsdp: 4 (over y).
Axes of the slice: x: 4, y: 4, z: 16, core: 2. Of those that a mesh axis runs over, the one named last changes fastest.
Arguments:
- query_key: bfloat16 [131072, 3072], P(('seq', 'fsdp')), may hold values from -48 to 48
- values: bfloat16 [131072, 3072], P(('seq', 'fsdp')), may hold values from -6 to 6
- cluster_ids: int32 [24, 1024], replicated, may hold values from 0 to 127, as said below
Outputs:
- attended: bfloat16 [131072, 3072], P(('seq', 'fsdp'))
Inputs may be any that keep to these rules, and one draw needn't show every extreme that they name: `cluster_ids`: for every head and cluster at most 10 blocks name that cluster, and for every head some cluster is named by exactly 10 blocks. Among the (head, block) pairs of one group of 6 consecutive heads and one run of 8 blocks starting at a multiple of 8, no cluster is named more than 1 times, and some cluster exactly 1 times; the blocks of one such run name distinct clusters for each head.
All inputs are finite; a program needn't handle non-finite values.
Results may differ from a plain program's by a relative error of at most 0.0027.
Values may be sent and summed in bfloat16 or wider, within the bound.
No kernel may reach another device: no remote copies, remote signals or barrier semaphores. Data moves between devices by JAX's collectives and lax.ppermute only.
A program may use at most 64 MiB of HBM per device.

v0:
```python
import math
import jax
import jax.numpy as jnp
from jax import lax
from jax.sharding import PartitionSpec as P

BLK = 128
masked_score = -1e30


def by_index(source_table, row_index):
    padded = jnp.concatenate(
        [source_table, jnp.zeros((1,) + source_table.shape[1:], source_table.dtype)], axis=0
    )
    return padded[row_index]


def softmax_group(key_rows, positions, alive_rows, score_scale):
    half = BLK // 2
    blocks = key_rows.shape[0] // BLK

    def by_half(rows):
        shaped = rows.reshape((blocks, 2, half) + rows.shape[1:])
        return jnp.swapaxes(shaped, 0, 1).reshape(rows.shape)

    query_rows = by_half(key_rows)
    query_positions = by_half(positions)
    query_alive = by_half(alive_rows)
    scores = jnp.dot(query_rows, key_rows.T, preferred_element_type=jnp.float32) * score_scale
    allowed = alive_rows[None, :] & (positions[None, :] <= query_positions[:, None])
    scores = jnp.where(allowed, scores, masked_score)
    row_peak = jnp.max(scores, axis=1, keepdims=True)
    weights = jnp.where(allowed, jnp.exp(scores - row_peak), 0.0)
    row_total = jnp.where(query_alive[:, None], jnp.sum(weights, axis=1, keepdims=True), 1.0)
    weights = weights.astype(jnp.bfloat16).reshape(2, blocks * half, key_rows.shape[0])
    row_total = row_total.reshape(2, blocks * half, 1)
    return (weights[0], weights[1], row_total[0], row_total[1])


def shards(query_key, values, cluster_ids):
    seq_count = lax.axis_size("seq")
    group_count = lax.axis_size("fsdp")
    seq_index = lax.axis_index("seq")
    group_index = lax.axis_index("fsdp")
    heads_all = cluster_ids.shape[0]
    group_heads = heads_all // group_count
    head_dim = query_key.shape[1] // heads_all
    tok_rows = query_key.shape[0]
    shard_blocks = group_count * tok_rows // BLK
    all_blocks = cluster_ids.shape[1]
    item_count = group_heads * shard_blocks
    slot_count = max(1, item_count // seq_count)
    capacity = shard_blocks + min(shard_blocks // 4, seq_count - shard_blocks)
    group_rows = capacity * BLK
    send_rows = seq_count * slot_count
    score_scale = 1.0 / math.sqrt(head_dim)
    keys_local, values_local = (
        lax.all_to_all(query_key, "fsdp", split_axis=1, concat_axis=0, tiled=True),
        lax.all_to_all(values, "fsdp", split_axis=1, concat_axis=0, tiled=True),
    )

    def into_items(block_data):
        shaped = block_data.reshape(shard_blocks, BLK, group_heads, head_dim)
        return jnp.transpose(shaped, (2, 0, 1, 3)).reshape(item_count, BLK, head_dim)

    key_items = into_items(keys_local)
    value_items = into_items(values_local)
    group_ids = lax.dynamic_slice_in_dim(cluster_ids, group_index * group_heads, group_heads, 0)
    by_source = jnp.transpose(
        group_ids.reshape(group_heads, seq_count, shard_blocks), (1, 0, 2)
    ).reshape(seq_count, item_count)
    own_dest = lax.dynamic_index_in_dim(by_source, seq_index, 0, keepdims=False)
    item_ids = jnp.arange(item_count, dtype=jnp.int32)
    earlier = (own_dest[None, :] == own_dest[:, None]) & (item_ids[None, :] < item_ids[:, None])
    own_pos = own_dest * slot_count + jnp.sum(earlier.astype(jnp.int32), axis=1)
    row_ids = jnp.arange(send_rows, dtype=jnp.int32)
    slot_match = own_pos[None, :] == row_ids[:, None]
    send_pick = jnp.sum(jnp.where(slot_match, item_ids[None, :], 0), axis=1) + item_count * (
        1 - jnp.any(slot_match, axis=1).astype(jnp.int32)
    )
    received_mask = (by_source == seq_index).astype(jnp.int32)
    recv_pos = (
        jnp.arange(seq_count, dtype=jnp.int32)[:, None] * slot_count
        + jnp.cumsum(received_mask, axis=1)
        - received_mask
    )
    recv_by_head = jnp.transpose(
        recv_pos.reshape(seq_count, group_heads, shard_blocks), (1, 0, 2)
    ).reshape(group_heads * all_blocks)
    owned_mask = (group_ids == seq_index).astype(jnp.int32)
    ordinal = jnp.cumsum(owned_mask, axis=1) - owned_mask
    target = jnp.where(
        owned_mask > 0, jnp.arange(group_heads, dtype=jnp.int32)[:, None] * capacity + ordinal, -1
    ).reshape(group_heads * all_blocks)
    slot_ids = jnp.arange(group_heads * capacity, dtype=jnp.int32)
    matches = target[None, :] == slot_ids[:, None]
    present = jnp.any(matches, axis=1)
    source_row = jnp.sum(jnp.where(matches, recv_by_head[None, :], 0), axis=1) + send_rows * (
        1 - present.astype(jnp.int32)
    )
    block_ids = jnp.tile(jnp.arange(all_blocks, dtype=jnp.int32), group_heads)
    block_of = jnp.sum(jnp.where(matches, block_ids[None, :], 0), axis=1)
    arrived_k = lax.all_to_all(
        by_index(key_items, send_pick), "seq", split_axis=0, concat_axis=0, tiled=True
    )
    arrived_v = lax.all_to_all(
        by_index(value_items, send_pick), "seq", split_axis=0, concat_axis=0, tiled=True
    )
    key_grouped = by_index(arrived_k, source_row)
    value_grouped = by_index(arrived_v, source_row)
    positions = (block_of[:, None] * BLK + jnp.arange(BLK, dtype=jnp.int32)[None, :]).reshape(
        group_heads, group_rows
    )
    alive_rows = jnp.repeat(present, BLK).reshape(group_heads, group_rows)

    def one_head(operands):
        key_rows, where_at, alive_here = operands
        return softmax_group(key_rows, where_at, alive_here, score_scale)

    weights_0, weights_1, totals_0, totals_1 = lax.map(
        one_head, (key_grouped.reshape(group_heads, group_rows, head_dim), positions, alive_rows)
    )
    half = BLK // 2
    value_rows = value_grouped.reshape(group_heads, group_rows, head_dim)
    back_match = source_row[None, :] == row_ids[:, None]
    back_pick = jnp.sum(
        jnp.where(back_match, slot_ids[None, :], 0), axis=1
    ) + group_heads * capacity * (1 - jnp.any(back_match, axis=1).astype(jnp.int32))
    pieces = []
    for part in range(2):
        part_weights = (weights_0, weights_1)[part]
        weighted = jnp.einsum(
            "hqk,hkd->hqd", part_weights, value_rows, preferred_element_type=jnp.float32
        )
        part_total = (totals_0, totals_1)[part]
        outputs = (weighted / part_total).astype(jnp.bfloat16)
        outputs = outputs.reshape(group_heads * capacity, half, head_dim)
        returned = lax.all_to_all(
            by_index(outputs, back_pick), "seq", split_axis=0, concat_axis=0, tiled=True
        )
        own_output = by_index(returned, own_pos)
        token_major = jnp.transpose(
            own_output.reshape(group_heads, shard_blocks, half, head_dim), (1, 2, 0, 3)
        ).reshape(shard_blocks * half, group_heads * head_dim)
        pieces.append(lax.all_to_all(token_major, "fsdp", split_axis=0, concat_axis=1, tiled=True))
    own_blocks = tok_rows // BLK
    joined = jnp.stack(
        [piece.reshape(own_blocks, half, heads_all * head_dim) for piece in pieces], axis=1
    )
    return joined.reshape(tok_rows, heads_all * head_dim)


def solution(mesh):
    placed = (P(("seq", "fsdp"), None), P(("seq", "fsdp"), None), P())
    return jax.shard_map(
        shards, mesh=mesh, in_specs=placed, out_specs=P(("seq", "fsdp"), None), check_vma=False
    )
```

profile of v0, /device:TPU:32, one launch (start us, length us, event | category | flops | bytes accessed | tf_op | source)
XLA Modules:
  0.0 725.8 jit_solution(8790920589746454872)
XLA Ops:
  0.0 2.6 copy.104
  2.6 4.6 all-to-all-start
  20.4 7.5 %all-to-all-done = bf16[256,4,768]{0,2,1:T(8,128)(2,1)S(1)} async-done(((bf16[256,4,768]{0,2,1:T(8,128)(2,1)}), bf16[256,4,768]{0,2,1:T(8,128)(2,1)S(1)}, u32[]{:S(2)}, u32[]{:S(2)}) %all-to-all-start) | async-done | bytes 1572896 | tf_op jit(solution)/shard_map/all_to_all | solution.py:58
  27.9 3.6 all-to-all-start.2
  34.8 2.5 reshape.280
  40.7 3.1 gather_fusion
  43.8 7.5 %all-to-all-done.2 = bf16[256,4,768]{0,2,1:T(8,128)(2,1)S(1)} async-done(((bf16[256,4,768]{0,2,1:T(8,128)(2,1)}), bf16[256,4,768]{0,2,1:T(8,128)(2,1)S(1)}, u32[]{:S(2)}, u32[]{:S(2)}) %all-to-all-start.2) | async-done | bytes 1572896 | tf_op jit(solution)/shard_map/all_to_all | solution.py:59
  51.3 19.5 %all-to-all-start.1 = ((bf16[128,128,128]{2,1,0:T(8,128)(2,1)}), bf16[128,128,128]{2,1,0:T(8,128)(2,1)}, u32[]{:S(2)}, u32[]{:S(2)}) async-start(bf16[128,128,128]{2,1,0:T(8,128)(2,1)} %gather_fusion), calls=%async_computation.1 | async-start | bytes 8388608 | tf_op jit(solution)/shard_map/all_to_all | solution.py:103
  76.1 3.1 gather_fusion.2
  79.2 179.2 %all-to-all-done.1 = bf16[128,128,128]{2,1,0:T(8,128)(2,1)} async-done(((bf16[128,128,128]{2,1,0:T(8,128)(2,1)}), bf16[128,128,128]{2,1,0:T(8,128)(2,1)}, u32[]{:S(2)}, u32[]{:S(2)}) %all-to-all-start.1) | async-done | bytes 4194336 | tf_op jit(solution)/shard_map/all_to_all | solution.py:103
  258.4 9.4 %all-to-all-start.3 = ((bf16[128,128,128]{2,1,0:T(8,128)(2,1)}), bf16[128,128,128]{2,1,0:T(8,128)(2,1)}, u32[]{:S(2)}, u32[]{:S(2)}) async-start(bf16[128,128,128]{2,1,0:T(8,128)(2,1)} %gather_fusion.2), calls=%async_computation.3 | async-start | bytes 8388608 | tf_op jit(solution)/shard_map/all_to_all | solution.py:106
  268.3 5.8 concatenate.25
  274.1 3.1 gather_fusion.1
  277.3 41.2 %while.16 = (s32[]{:T(128)}, bf16[6,640,1280]{1,2,0:T(8,128)(2,1)}, bf16[6,640,1280]{1,2,0:T(8,128)(2,1)}, f32[6,640,1]{1,0,2:T(8,128)S(1)}, f32[6,640,1]{1,0,2:...) while((s32[]{:T(128)}, bf16[6,640,1280]{1,2,0:T(8,128)(2,1)}, ...), condition=%wide.region_12.13_spmd, body=%wide.region_9.12_spmd.sunk | while | flops 437451520 | bytes 25025912 | solution.py:120
  279.3 2.4 fusion.30
  286.2 2.4 fusion.30
  293.1 2.4 fusion.30
  299.9 2.4 fusion.30
  306.8 2.4 fusion.30
  318.5 137.1 %all-to-all-done.3 = bf16[128,128,128]{2,1,0:T(8,128)(2,1)} async-done(((bf16[128,128,128]{2,1,0:T(8,128)(2,1)}), bf16[128,128,128]{2,1,0:T(8,128)(2,1)}, u32[]{:S(2)}, u32[]{:S(2)}) %all-to-all-start.3) | async-done | bytes 4194336 | tf_op jit(solution)/shard_map/all_to_all | solution.py:106
  455.5 5.8 concatenate.27
  461.3 3.1 gather_fusion.3
  464.5 7.7 %divide_convert_fusion.1 = bf16[6,640,128]{2,1,0:T(8,128)(2,1)S(1)} fusion(f32[6,640]{1,0:T(8,128)S(1)} %bitcast.151, bf16[6,640,1280]{1,2,0:T(8,128)(2,1)} %get-tuple-element.50, bf16[6,1280,128]{2,1,0:T(8,128)(2,1)S(1)} %bitcast.140), kind=kOutput, calls=%fused_computation.26 | convolution fusion | flops 1259274240 | bytes 12794880 | tf_op jit(solution)/shard_map/hqk,hkd->hqd/dot_general | solution.py:132
  474.5 8.9 %all-to-all-start.4 = ((bf16[128,64,128]{2,1,0:T(8,128)(2,1)}), bf16[128,64,128]{2,1,0:T(8,128)(2,1)S(1)}, u32[]{:S(2)}, u32[]{:S(2)}) async-start(bf16[128,64,128]{2,1,0:T(8,128)(2,1)} %gather_fusion.4), calls=%async_computation.4 | async-start | bytes 4194304 | tf_op jit(solution)/shard_map/all_to_all | solution.py:138
  483.4 7.6 %divide_convert_fusion = bf16[6,640,128]{2,1,0:T(8,128)(2,1)S(1)} fusion(f32[6,640]{1,0:T(8,128)S(1)} %bitcast.152, bf16[6,640,1280]{1,2,0:T(8,128)(2,1)} %get-tuple-element.52, bf16[6,1280,128]{2,1,0:T(8,128)(2,1)} %bitcast.141), kind=kOutput, calls=%fused_computation.25 | convolution fusion | flops 1259274240 | bytes 12794880 | tf_op jit(solution)/shard_map/hqk,hkd->hqd/dot_general | solution.py:132
  493.2 88.5 %all-to-all-done.4 = bf16[128,64,128]{2,1,0:T(8,128)(2,1)S(1)} async-done(((bf16[128,64,128]{2,1,0:T(8,128)(2,1)}), bf16[128,64,128]{2,1,0:T(8,128)(2,1)S(1)}, u32[]{:S(2)}, u32[]{:S(2)}) %all-to-all-start.4) | async-done | bytes 2097184 | tf_op jit(solution)/shard_map/all_to_all | solution.py:138
  581.7 9.1 %all-to-all-start.6 = ((bf16[128,64,128]{2,1,0:T(8,128)(2,1)}), bf16[128,64,128]{2,1,0:T(8,128)(2,1)}, u32[]{:S(2)}, u32[]{:S(2)}) async-start(bf16[128,64,128]{2,1,0:T(8,128)(2,1)} %gather_fusion.6), calls=%async_computation.6 | async-start | bytes 4194304 | tf_op jit(solution)/shard_map/all_to_all | solution.py:138
  597.3 91.5 %all-to-all-done.6 = bf16[128,64,128]{2,1,0:T(8,128)(2,1)} async-done(((bf16[128,64,128]{2,1,0:T(8,128)(2,1)}), bf16[128,64,128]{2,1,0:T(8,128)(2,1)}, u32[]{:S(2)}, u32[]{:S(2)}) %all-to-all-start.6) | async-done | bytes 2097184 | tf_op jit(solution)/shard_map/all_to_all | solution.py:138
  688.8 4.2 all-to-all-start.5
  698.0 8.4 %all-to-all-done.5 = bf16[4,128,768]{2,1,0:T(8,128)(2,1)} async-done(((bf16[4,128,768]{2,1,0:T(8,128)(2,1)}), bf16[4,128,768]{2,1,0:T(8,128)(2,1)}, u32[]{:S(2)}, u32[]{:S(2)}) %all-to-all-start.5) | async-done | bytes 786464 | tf_op jit(solution)/shard_map/all_to_all | solution.py:145
  706.5 3.7 all-to-all-start.7
  712.5 10.5 %all-to-all-done.7 = bf16[4,128,768]{2,1,0:T(8,128)(2,1)S(1)} async-done(((bf16[4,128,768]{2,1,0:T(8,128)(2,1)}), bf16[4,128,768]{2,1,0:T(8,128)(2,1)S(1)}, u32[]{:S(2)}, u32[]{:S(2)}) %all-to-all-start.7) | async-done | bytes 786464 | tf_op jit(solution)/shard_map/all_to_all | solution.py:145
  (180 shorter events, 75.1 us)
Async XLA Ops:
  2.6 15.8 %copy-start.1 = (bf16[256,3072]{1,0:T(8,128)(2,1)S(1)}, bf16[256,3072]{1,0:T(8,128)(2,1)}, u32[]{:S(2)}) copy-start(bf16[256,3072]{1,0:T(8,128)(2,1)} %param.6) | copy-start | bytes 4718596
  2.6 25.3 %all-to-all-start = ((bf16[256,4,768]{0,2,1:T(8,128)(2,1)}), bf16[256,4,768]{0,2,1:T(8,128)(2,1)S(1)}, u32[]{:S(2)}, u32[]{:S(2)}) async-start(bf16[256,4,768]{0,2,1:T(8,128)(2,1)} %bitcast.13), calls=%async_computation | async-start | bytes 3145728 | tf_op jit(solution)/shard_map/all_to_all | solution.py:58
  17.1 2.9 copy-start.2
  17.1 3.1 copy-start.3
  20.0 11.5 %copy-start.4 = (s32[6144]{0:T(1024)S(1)}, s32[6144]{0:T(1024)}, u32[]{:S(2)}) copy-start(s32[6144]{0:T(1024)} %broadcast_in_dim.110) | copy-start | bytes 73732
  27.9 23.4 %all-to-all-start.2 = ((bf16[256,4,768]{0,2,1:T(8,128)(2,1)}), bf16[256,4,768]{0,2,1:T(8,128)(2,1)S(1)}, u32[]{:S(2)}, u32[]{:S(2)}) async-start(bf16[256,4,768]{0,2,1:T(8,128)(2,1)} %bitcast.132), calls=%async_computation.2 | async-start | bytes 3145728 | tf_op jit(solution)/shard_map/all_to_all | solution.py:59
  51.3 207.2 %all-to-all-start.1 = ((bf16[128,128,128]{2,1,0:T(8,128)(2,1)}), bf16[128,128,128]{2,1,0:T(8,128)(2,1)}, u32[]{:S(2)}, u32[]{:S(2)}) async-start(bf16[128,128,128]{2,1,0:T(8,128)(2,1)} %gather_fusion), calls=%async_computation.1 | async-start | bytes 8388608 | tf_op jit(solution)/shard_map/all_to_all | solution.py:103
  258.4 197.1 %all-to-all-start.3 = ((bf16[128,128,128]{2,1,0:T(8,128)(2,1)}), bf16[128,128,128]{2,1,0:T(8,128)(2,1)}, u32[]{:S(2)}, u32[]{:S(2)}) async-start(bf16[128,128,128]{2,1,0:T(8,128)(2,1)} %gather_fusion.2), calls=%async_computation.3 | async-start | bytes 8388608 | tf_op jit(solution)/shard_map/all_to_all | solution.py:106
  464.5 7.8 %copy-start = (bf16[60,128,128]{2,1,0:T(8,128)(2,1)}, bf16[60,128,128]{2,1,0:T(8,128)(2,1)S(1)}, u32[]{:S(2)}) copy-start(bf16[60,128,128]{2,1,0:T(8,128)(2,1)S(1)} %gather_fusion.3) | copy-start | bytes 5898244
  474.5 107.2 %all-to-all-start.4 = ((bf16[128,64,128]{2,1,0:T(8,128)(2,1)}), bf16[128,64,128]{2,1,0:T(8,128)(2,1)S(1)}, u32[]{:S(2)}, u32[]{:S(2)}) async-start(bf16[128,64,128]{2,1,0:T(8,128)(2,1)} %gather_fusion.4), calls=%async_computation.4 | async-start | bytes 4194304 | tf_op jit(solution)/shard_map/all_to_all | solution.py:138
  581.7 107.1 %all-to-all-start.6 = ((bf16[128,64,128]{2,1,0:T(8,128)(2,1)}), bf16[128,64,128]{2,1,0:T(8,128)(2,1)}, u32[]{:S(2)}, u32[]{:S(2)}) async-start(bf16[128,64,128]{2,1,0:T(8,128)(2,1)} %gather_fusion.6), calls=%async_computation.6 | async-start | bytes 4194304 | tf_op jit(solution)/shard_map/all_to_all | solution.py:138
  688.8 17.7 %all-to-all-start.5 = ((bf16[4,128,768]{2,1,0:T(8,128)(2,1)}), bf16[4,128,768]{2,1,0:T(8,128)(2,1)}, u32[]{:S(2)}, u32[]{:S(2)}) async-start(bf16[4,128,768]{2,1,0:T(8,128)(2,1)} %all_to_all.69), calls=%async_computation.5 | async-start | bytes 1572864 | tf_op jit(solution)/shard_map/all_to_all | solution.py:145
  706.5 16.5 %all-to-all-start.7 = ((bf16[4,128,768]{2,1,0:T(8,128)(2,1)}), bf16[4,128,768]{2,1,0:T(8,128)(2,1)S(1)}, u32[]{:S(2)}, u32[]{:S(2)}) async-start(bf16[4,128,768]{2,1,0:T(8,128)(2,1)} %all_to_all.73), calls=%async_computation.7 | async-start | bytes 1572864 | tf_op jit(solution)/shard_map/all_to_all | solution.py:145
where the time goes:
time: 735 us; the launch traced here: 726 us
  waiting for transfers between devices  530 us (72%)
  local copies, waits for them, and re-layouts  83.8 us (11%)
  starting transfers between devices  62.9 us (9%)
  matrix products  25.9 us (4%)
  other arithmetic  22 us (3%)
    all_to_all x2, waiting for transfers between devices, shards(): lax.all_to_all(by_index(outputs, back_pick), 'seq', split_axis=0, concat_...  180 us
    all_to_all x1, waiting for transfers between devices, shards(): lax.all_to_all(by_index(key_items, send_pick), 'seq', split_axis=0, conca...  179 us
    all_to_all x1, waiting for transfers between devices, shards(): lax.all_to_all(by_index(value_items, send_pick), 'seq', split_axis=0, con...  137 us
    gather x8, local copies, waits for them, and re-layouts, by_index(): return padded[row_index]  19.8 us
    all_to_all x1, starting transfers between devices, shards(): lax.all_to_all(by_index(key_items, send_pick), 'seq', split_axis=0, conca...  19.5 us
    all_to_all x2, waiting for transfers between devices, shards(): lax.all_to_all(token_major, 'fsdp', split_axis=0, concat_axis=1, tiled=True)  18.9 us
    concatenate x8, local copies, waits for them, and re-layouts, by_index(): jnp.concatenate([source_table, jnp.zeros((1,) + source_table.shape[1:], s...  18.7 us
    all_to_all x2, starting transfers between devices, shards(): lax.all_to_all(by_index(outputs, back_pick), 'seq', split_axis=0, concat_...  18 us
  transfers between devices with their start and end apart: 8, of which 8 were waited for; matrix products, arithmetic and copies ran while one was open for 14% of the time, Pallas kernels for 0%

commit v1 on v0

--- a/solution.py
+++ b/solution.py
@@ -142,7 +142,14 @@
         token_major = jnp.transpose(
             own_output.reshape(group_heads, shard_blocks, half, head_dim), (1, 2, 0, 3)
         ).reshape(shard_blocks * half, group_heads * head_dim)
-        pieces.append(lax.all_to_all(token_major, "fsdp", split_axis=0, concat_axis=1, tiled=True))
+        pieces.append(
+            jnp.concatenate(
+                lax.all_to_all(
+                    jnp.stack(jnp.split(token_major, lax.axis_size("fsdp"), axis=0)), "fsdp", 0, 0
+                ),
+                axis=1,
+            )
+        )
     own_blocks = tok_rows // BLK
     joined = jnp.stack(
         [piece.reshape(own_blocks, half, heads_all * head_dim) for piece in pieces], axis=1

time: 735 us -> 736 us (level)
  transfers between devices with their start and end apart: 8 -> 8, of which waited for: 8 -> 8; matrix products, arithmetic and copies ran while one was open for 14% -> 15% of each run, Pallas kernels for 0% -> 0%
where the time goes in v1:
time: 736 us; the launch traced here: 726 us
  waiting for transfers between devices  528 us (72%)
  local copies, waits for them, and re-layouts  85.5 us (12%)
  starting transfers between devices  61.7 us (8%)
  matrix products  25.9 us (4%)
  other arithmetic  24 us (3%)
    all_to_all x1, waiting for transfers between devices, shards(): lax.all_to_all(by_index(key_items, send_pick), 'seq', split_axis=0, conca...  179 us
    all_to_all x2, waiting for transfers between devices, shards(): lax.all_to_all(by_index(outputs, back_pick), 'seq', split_axis=0, concat_...  179 us
    all_to_all x1, waiting for transfers between devices, shards(): lax.all_to_all(by_index(value_items, send_pick), 'seq', split_axis=0, con...  137 us
    gather x8, local copies, waits for them, and re-layouts, by_index(): return padded[row_index]  21.4 us
    concatenate x8, local copies, waits for them, and re-layouts, by_index(): jnp.concatenate([source_table, jnp.zeros((1,) + source_table.shape[1:], s...  20 us
    all_to_all x1, starting transfers between devices, shards(): lax.all_to_all(by_index(key_items, send_pick), 'seq', split_axis=0, conca...  19.5 us
    all_to_all x2, waiting for transfers between devices, shards(): lax.all_to_all(jnp.stack(jnp.split(token_major, lax.axis_size('fsdp'), ax...  18.3 us
    all_to_all x2, starting transfers between devices, shards(): lax.all_to_all(by_index(outputs, back_pick), 'seq', split_axis=0, concat_...  17.5 us
  transfers between devices with their start and end apart: 8, of which 8 were waited for; matrix products, arithmetic and copies ran while one was open for 15% of the time, Pallas kernels for 0%

profile of v1, /device:TPU:32, one launch (start us, length us, event | category | flops | bytes accessed | tf_op | source)
XLA Modules:
  0.0 726.3 jit_solution(9864927185608770934)
XLA Ops:
  0.0 2.6 copy.128
  2.6 4.6 all-to-all-start
  20.4 7.5 %all-to-all-done = bf16[256,4,768]{0,2,1:T(8,128)(2,1)S(1)} async-done(((bf16[256,4,768]{0,2,1:T(8,128)(2,1)}), bf16[256,4,768]{0,2,1:T(8,128)(2,1)S(1)}, u32[]{:S(2)}, u32[]{:S(2)}) %all-to-all-start) | async-done | bytes 1572896 | tf_op jit(solution)/shard_map/all_to_all | solution.py:58
  27.9 3.6 all-to-all-start.2
  34.8 2.5 reshape.292
  40.7 3.1 gather_fusion
  43.8 7.5 %all-to-all-done.2 = bf16[256,4,768]{0,2,1:T(8,128)(2,1)S(1)} async-done(((bf16[256,4,768]{0,2,1:T(8,128)(2,1)}), bf16[256,4,768]{0,2,1:T(8,128)(2,1)S(1)}, u32[]{:S(2)}, u32[]{:S(2)}) %all-to-all-start.2) | async-done | bytes 1572896 | tf_op jit(solution)/shard_map/all_to_all | solution.py:59
  51.3 19.5 %all-to-all-start.1 = ((bf16[128,128,128]{2,1,0:T(8,128)(2,1)}), bf16[128,128,128]{2,1,0:T(8,128)(2,1)}, u32[]{:S(2)}, u32[]{:S(2)}) async-start(bf16[128,128,128]{2,1,0:T(8,128)(2,1)} %gather_fusion), calls=%async_computation.1 | async-start | bytes 8388608 | tf_op jit(solution)/shard_map/all_to_all | solution.py:103
  76.1 3.1 gather_fusion.2
  79.2 179.2 %all-to-all-done.1 = bf16[128,128,128]{2,1,0:T(8,128)(2,1)} async-done(((bf16[128,128,128]{2,1,0:T(8,128)(2,1)}), bf16[128,128,128]{2,1,0:T(8,128)(2,1)}, u32[]{:S(2)}, u32[]{:S(2)}) %all-to-all-start.1) | async-done | bytes 4194336 | tf_op jit(solution)/shard_map/all_to_all | solution.py:103
  258.4 9.4 %all-to-all-start.3 = ((bf16[128,128,128]{2,1,0:T(8,128)(2,1)}), bf16[128,128,128]{2,1,0:T(8,128)(2,1)}, u32[]{:S(2)}, u32[]{:S(2)}) async-start(bf16[128,128,128]{2,1,0:T(8,128)(2,1)} %gather_fusion.2), calls=%async_computation.3 | async-start | bytes 8388608 | tf_op jit(solution)/shard_map/all_to_all | solution.py:106
  268.3 5.8 concatenate.25
  274.1 3.1 gather_fusion.1
  277.3 41.2 %while.16 = (s32[]{:T(128)}, bf16[6,640,1280]{1,2,0:T(8,128)(2,1)}, bf16[6,640,1280]{1,2,0:T(8,128)(2,1)}, f32[6,640,1]{1,0,2:T(8,128)S(1)}, f32[6,640,1]{1,0,2:...) while((s32[]{:T(128)}, bf16[6,640,1280]{1,2,0:T(8,128)(2,1)}, ...), condition=%wide.region_12.13_spmd, body=%wide.region_9.12_spmd.sunk | while | flops 437451520 | bytes 25025912 | solution.py:120
  279.3 2.4 fusion.32
  286.2 2.4 fusion.32
  293.1 2.4 fusion.32
  299.9 2.4 fusion.32
  318.5 137.1 %all-to-all-done.3 = bf16[128,128,128]{2,1,0:T(8,128)(2,1)} async-done(((bf16[128,128,128]{2,1,0:T(8,128)(2,1)}), bf16[128,128,128]{2,1,0:T(8,128)(2,1)}, u32[]{:S(2)}, u32[]{:S(2)}) %all-to-all-start.3) | async-done | bytes 4194336 | tf_op jit(solution)/shard_map/all_to_all | solution.py:106
  455.5 5.8 concatenate.27
  461.3 3.1 gather_fusion.3
  464.5 7.7 %divide_convert_fusion.1 = bf16[6,640,128]{2,1,0:T(8,128)(2,1)S(1)} fusion(f32[6,640]{1,0:T(8,128)S(1)} %bitcast.152, bf16[6,640,1280]{1,2,0:T(8,128)(2,1)} %get-tuple-element.50, bf16[6,1280,128]{2,1,0:T(8,128)(2,1)S(1)} %bitcast.141), kind=kOutput, calls=%fused_computation.26 | convolution fusion | flops 1259274240 | bytes 12794880 | tf_op jit(solution)/shard_map/hqk,hkd->hqd/dot_general | solution.py:132
  474.5 8.9 %all-to-all-start.4 = ((bf16[128,64,128]{2,1,0:T(8,128)(2,1)}), bf16[128,64,128]{2,1,0:T(8,128)(2,1)S(1)}, u32[]{:S(2)}, u32[]{:S(2)}) async-start(bf16[128,64,128]{2,1,0:T(8,128)(2,1)} %gather_fusion.4), calls=%async_computation.4 | async-start | bytes 4194304 | tf_op jit(solution)/shard_map/all_to_all | solution.py:138
  483.4 7.6 %divide_convert_fusion = bf16[6,640,128]{2,1,0:T(8,128)(2,1)S(1)} fusion(f32[6,640]{1,0:T(8,128)S(1)} %bitcast.153, bf16[6,640,1280]{1,2,0:T(8,128)(2,1)} %get-tuple-element.52, bf16[6,1280,128]{2,1,0:T(8,128)(2,1)} %bitcast.142), kind=kOutput, calls=%fused_computation.25 | convolution fusion | flops 1259274240 | bytes 12794880 | tf_op jit(solution)/shard_map/hqk,hkd->hqd/dot_general | solution.py:132
  493.2 88.5 %all-to-all-done.4 = bf16[128,64,128]{2,1,0:T(8,128)(2,1)S(1)} async-done(((bf16[128,64,128]{2,1,0:T(8,128)(2,1)}), bf16[128,64,128]{2,1,0:T(8,128)(2,1)S(1)}, u32[]{:S(2)}, u32[]{:S(2)}) %all-to-all-start.4) | async-done | bytes 2097184 | tf_op jit(solution)/shard_map/all_to_all | solution.py:138
  583.1 8.6 %all-to-all-start.6 = ((bf16[128,64,128]{2,1,0:T(8,128)(2,1)}), bf16[128,64,128]{2,1,0:T(8,128)(2,1)S(1)}, u32[]{:S(2)}, u32[]{:S(2)}) async-start(bf16[128,64,128]{2,1,0:T(8,128)(2,1)} %gather_fusion.6), calls=%async_computation.6 | async-start | bytes 4194304 | tf_op jit(solution)/shard_map/all_to_all | solution.py:138
  591.7 3.4 concatenate.29
  600.0 90.0 %all-to-all-done.6 = bf16[128,64,128]{2,1,0:T(8,128)(2,1)S(1)} async-done(((bf16[128,64,128]{2,1,0:T(8,128)(2,1)}), bf16[128,64,128]{2,1,0:T(8,128)(2,1)S(1)}, u32[]{:S(2)}, u32[]{:S(2)}) %all-to-all-start.6) | async-done | bytes 2097184 | tf_op jit(solution)/shard_map/all_to_all | solution.py:138
  690.0 3.5 all-to-all-start.5
  700.2 6.7 all-to-all-done.5
  706.9 3.7 all-to-all-start.7
  711.8 11.6 %all-to-all-done.7 = bf16[4,128,768]{2,1,0:T(8,128)(2,1)S(1)} async-done(((bf16[4,128,768]{2,1,0:T(8,128)(2,1)}), bf16[4,128,768]{2,1,0:T(8,128)(2,1)S(1)}, u32[]{:S(2)}, u32[]{:S(2)}) %all-to-all-start.7) | async-done | bytes 786464 | tf_op jit(solution)/shard_map/all_to_all | solution.py:147
  (198 shorter events, 77.8 us)
Async XLA Ops:
  2.6 15.8 %copy-start.2 = (bf16[256,3072]{1,0:T(8,128)(2,1)S(1)}, bf16[256,3072]{1,0:T(8,128)(2,1)}, u32[]{:S(2)}) copy-start(bf16[256,3072]{1,0:T(8,128)(2,1)} %param.6) | copy-start | bytes 4718596
  2.6 25.3 %all-to-all-start = ((bf16[256,4,768]{0,2,1:T(8,128)(2,1)}), bf16[256,4,768]{0,2,1:T(8,128)(2,1)S(1)}, u32[]{:S(2)}, u32[]{:S(2)}) async-start(bf16[256,4,768]{0,2,1:T(8,128)(2,1)} %bitcast.13), calls=%async_computation | async-start | bytes 3145728 | tf_op jit(solution)/shard_map/all_to_all | solution.py:58
  17.1 2.9 copy-start.3
  17.1 3.1 copy-start.4
  20.0 11.5 %copy-start.5 = (s32[6144]{0:T(1024)S(1)}, s32[6144]{0:T(1024)}, u32[]{:S(2)}) copy-start(s32[6144]{0:T(1024)} %broadcast_in_dim.110) | copy-start | bytes 73732
  27.9 23.4 %all-to-all-start.2 = ((bf16[256,4,768]{0,2,1:T(8,128)(2,1)}), bf16[256,4,768]{0,2,1:T(8,128)(2,1)S(1)}, u32[]{:S(2)}, u32[]{:S(2)}) async-start(bf16[256,4,768]{0,2,1:T(8,128)(2,1)} %bitcast.132), calls=%async_computation.2 | async-start | bytes 3145728 | tf_op jit(solution)/shard_map/all_to_all | solution.py:59
  51.3 207.2 %all-to-all-start.1 = ((bf16[128,128,128]{2,1,0:T(8,128)(2,1)}), bf16[128,128,128]{2,1,0:T(8,128)(2,1)}, u32[]{:S(2)}, u32[]{:S(2)}) async-start(bf16[128,128,128]{2,1,0:T(8,128)(2,1)} %gather_fusion), calls=%async_computation.1 | async-start | bytes 8388608 | tf_op jit(solution)/shard_map/all_to_all | solution.py:103
  258.4 197.1 %all-to-all-start.3 = ((bf16[128,128,128]{2,1,0:T(8,128)(2,1)}), bf16[128,128,128]{2,1,0:T(8,128)(2,1)}, u32[]{:S(2)}, u32[]{:S(2)}) async-start(bf16[128,128,128]{2,1,0:T(8,128)(2,1)} %gather_fusion.2), calls=%async_computation.3 | async-start | bytes 8388608 | tf_op jit(solution)/shard_map/all_to_all | solution.py:106
  464.5 7.8 %copy-start.1 = (bf16[60,128,128]{2,1,0:T(8,128)(2,1)}, bf16[60,128,128]{2,1,0:T(8,128)(2,1)S(1)}, u32[]{:S(2)}) copy-start(bf16[60,128,128]{2,1,0:T(8,128)(2,1)S(1)} %gather_fusion.3) | copy-start | bytes 5898244
  474.5 107.2 %all-to-all-start.4 = ((bf16[128,64,128]{2,1,0:T(8,128)(2,1)}), bf16[128,64,128]{2,1,0:T(8,128)(2,1)S(1)}, u32[]{:S(2)}, u32[]{:S(2)}) async-start(bf16[128,64,128]{2,1,0:T(8,128)(2,1)} %gather_fusion.4), calls=%async_computation.4 | async-start | bytes 4194304 | tf_op jit(solution)/shard_map/all_to_all | solution.py:138
  581.7 1.3 copy-start
  583.1 107.0 %all-to-all-start.6 = ((bf16[128,64,128]{2,1,0:T(8,128)(2,1)}), bf16[128,64,128]{2,1,0:T(8,128)(2,1)S(1)}, u32[]{:S(2)}, u32[]{:S(2)}) async-start(bf16[128,64,128]{2,1,0:T(8,128)(2,1)} %gather_fusion.6), calls=%async_computation.6 | async-start | bytes 4194304 | tf_op jit(solution)/shard_map/all_to_all | solution.py:138
  690.0 16.9 %all-to-all-start.5 = ((bf16[4,128,768]{2,1,0:T(8,128)(2,1)}), bf16[4,128,768]{2,1,0:T(8,128)(2,1)S(1)}, u32[]{:S(2)}, u32[]{:S(2)}) async-start(bf16[4,128,768]{2,1,0:T(8,128)(2,1)} %pad_maximum_fusion.1), calls=%async_computation.5 | async-start | bytes 1572864 | tf_op jit(solution)/shard_map/all_to_all | solution.py:147
  706.9 16.5 %all-to-all-start.7 = ((bf16[4,128,768]{2,1,0:T(8,128)(2,1)}), bf16[4,128,768]{2,1,0:T(8,128)(2,1)S(1)}, u32[]{:S(2)}, u32[]{:S(2)}) async-start(bf16[4,128,768]{2,1,0:T(8,128)(2,1)} %pad_maximum_fusion.2), calls=%async_computation.7 | async-start | bytes 1572864 | tf_op jit(solution)/shard_map/all_to_all | solution.py:147
